TPU v7x, 32 devices: a whole 2x2x4 slice. The times are simulated.
32 devices in a mesh: groups: 2 (over y), seq: 4 (over z), chan: 4 (over x, core).
Axes of the slice: x: 2, y: 2, z: 4, core: 2. Of those that a mesh axis runs over, the one named last changes fastest.
Arguments:
- value: bfloat16 [1024, 4096], P(('groups', 'seq'), 'chan'), parts along dimension 0, may hold values from -6 to 6
- first_gate: bfloat16 [1024, 4096], P(('groups', 'seq'), 'chan'), parts along dimension 0, may hold values from -6 to 6
- second_gate: bfloat16 [1024, 4096], P(('groups', 'seq'), 'chan'), parts along dimension 0, may hold values from -6 to 6
- first_filter: bfloat16 [256, 512], P('chan'), may hold values from -0.25 to 0.25
- second_filter: bfloat16 [256, 512], P('chan'), may hold values from -0.25 to 0.25
- out_weight: bfloat16 [4096, 4096], P('chan'), may hold values from -0.09375 to 0.09375
- segment_ids: int32 [1024], P(('groups', 'seq')), parts along dimension 0, may hold values from 0 to 1, never falling along the last dimension, each value on 1 to 384 neighbouring positions
Outputs:
- mixed: bfloat16 [1024, 4096], P(('groups', 'seq')), parts along dimension 0
There are 2 independent parts, one for each index of `groups`. A program takes and returns all parts, laid end to end along the dimension named above; an argument that names none is the same for every part. Nothing has to cross between parts.
Inputs may be any that keep to these rules, and one draw needn't show every extreme that they name: `segment_ids`: ids never fall along the window; the 2 contexts each hold 128 to 384 neighbouring positions and together fill the window.
All inputs are finite; a program needn't handle non-finite values.
Results may differ from a plain program's by a relative error of at most 0.0065.
Values may be sent and summed in bfloat16 or wider, within the bound.
No kernel may reach another device: no remote copies, remote signals or barrier semaphores. Data moves between devices by JAX's collectives and lax.ppermute only.
A program may use at most 192 MiB of HBM per device.

v0:
```python
import numpy as np
import jax
import jax.numpy as jnp
from jax import lax
from jax.sharding import PartitionSpec as P

F32 = jnp.float32
BF16 = jnp.bfloat16


def split_bf16(mat):
    hi = mat.astype(jnp.bfloat16)
    lo = (mat - hi.astype(np.float64)).astype(jnp.bfloat16)
    return (hi, lo)


def dft_mats(length):
    half = length // 2
    n = np.arange(length)
    f = np.arange(half)
    ang = 2.0 * np.pi * (f[:, None] * n[None, :] % length) / length
    fwd = np.zeros((length, length))
    fwd[:half] = np.cos(ang)
    fwd[half] = np.where(n % 2 == 0, 1.0, -1.0)
    fwd[half + 1 :] = -np.sin(ang[1:])
    inv = np.zeros((length, length))
    scale = np.full(half, 2.0)
    scale[0] = 1.0
    inv[:, :half] = (np.cos(ang) * scale[:, None]).T / length
    inv[:, half] = np.where(n % 2 == 0, 1.0, -1.0) / length
    inv[:, half + 1 :] = (-2.0 * np.sin(ang[1:])).T / length
    return (split_bf16(fwd), split_bf16(inv))


def mm(a, b):
    return jnp.dot(a, b, preferred_element_type=F32)


def swap(x, bit):
    return lax.ppermute(x, "chan", [(c, c ^ bit) for c in range(4)])


def make_local(nseq, nchan):

    def local(value, first_gate, second_gate, first_filter, second_filter, out_weight, segment_ids):
        chans = value.shape[1]
        filt_local, length = first_filter.shape
        group = chans // filt_local
        per = chans // nseq
        fpd = per // group
        half = length // 2
        (f_hi, f_lo), (i_hi, i_lo) = dft_mats(length)
        f_hi, f_lo, i_hi, i_lo = (jnp.asarray(m) for m in (f_hi, f_lo, i_hi, i_lo))
        me = lax.axis_index("seq")

        def spectrum(filt):
            mine = lax.dynamic_slice_in_dim(filt, me * fpd, fpd, 0)
            taps = jnp.repeat(mine.T, group, axis=1)
            spec = mm(f_hi, taps) + mm(f_lo, taps)
            re, im = (spec[:half], spec[half:])
            row0 = lax.broadcasted_iota(jnp.int32, re.shape, 0) == 0
            a = re
            b = jnp.where(row0, 0.0, im)
            d = jnp.where(row0, im, re)
            two = lambda x: jnp.concatenate([x, x], axis=1)
            return (two(a), two(b), two(d))

        def long_conv(spec, field):
            a, b, d = spec
            zero = jnp.zeros_like(field)
            masked = jnp.concatenate(
                [jnp.where(in0, field, zero), jnp.where(in1, field, zero)], axis=1
            )
            x = mm(f_hi, masked) + mm(f_lo, masked)
            xr, xi = (x[:half], x[half:])
            y = jnp.concatenate([xr * a - xi * b, xr * b + xi * d], axis=0)
            y_hi32 = lax.reduce_precision(y, exponent_bits=8, mantissa_bits=7)
            y_hi = y_hi32.astype(BF16)
            y_lo = (y - y_hi32).astype(BF16)
            both = mm(i_hi, y_hi) + mm(i_hi, y_lo) + mm(i_lo, y_hi)
            return jnp.where(in0, both[:, :per], 0.0) + jnp.where(in1, both[:, per:], 0.0)

        rows = value.shape[0]
        first_input = (first_gate.astype(F32) * value.astype(F32)).astype(BF16)
        first_input = first_input.reshape(rows, nseq, per).transpose(1, 0, 2)
        id_rows = -(-rows // per)
        pad_rows = -(-id_rows // 16) * 16
        ids = jnp.pad(segment_ids.astype(BF16), (0, pad_rows * per - rows)).reshape(
            1, pad_rows, per
        )
        payload = jnp.concatenate(
            [first_input, jnp.broadcast_to(ids, (nseq, pad_rows, per))], axis=1
        )
        got = lax.all_to_all(payload, "seq", 0, 0, tiled=True)
        first_cols = got[:, :rows].reshape(nseq * rows, per)
        segs = got[:, rows:].reshape(nseq, pad_rows * per)[:, :rows].reshape(nseq * rows)
        in0 = (segs == 0)[:, None]
        in1 = (segs == 1)[:, None]
        gate_blocks = second_gate.reshape(rows, nseq, per).transpose(1, 0, 2)
        gate_cols = lax.all_to_all(gate_blocks, "seq", 0, 0, tiled=True).reshape(nseq * rows, per)
        first_mix = long_conv(spectrum(first_filter), first_cols)
        second_input = (gate_cols.astype(F32) * first_mix).astype(BF16)
        second_mix = long_conv(spectrum(second_filter), second_input).astype(BF16)
        mix_blocks = lax.all_to_all(second_mix.reshape(nseq, rows, per), "seq", 0, 0, tiled=True)
        out_cols = out_weight.shape[1]
        w_blocks = out_weight.reshape(nseq, per, out_cols)

        def project(w):
            return lax.dot_general(
                mix_blocks, w, (((0, 2), (0, 1)), ((), ())), preferred_element_type=F32
            )

        if nchan != 4:
            return lax.psum(project(w_blocks), "chan").astype(BF16)
        core = lax.axis_index("chan") % 2
        width = out_cols // 2
        w_halves = w_blocks.reshape(nseq, per, 2, width)
        other = project(lax.dynamic_index_in_dim(w_halves, 1 - core, 2, keepdims=False))
        got_other = swap(other.astype(BF16), 1)
        mine = project(lax.dynamic_index_in_dim(w_halves, core, 2, keepdims=False))
        chip = mine + got_other.astype(F32)
        total = (chip + swap(chip.astype(BF16), 2).astype(F32)).astype(BF16)
        peer = swap(total, 1)
        return jnp.where(
            core == 0, jnp.concatenate([total, peer], 1), jnp.concatenate([peer, total], 1)
        )

    return local


def solution(mesh):
    in_specs = (
        P(("groups", "seq"), "chan"),
        P(("groups", "seq"), "chan"),
        P(("groups", "seq"), "chan"),
        P("chan", None),
        P("chan", None),
        P("chan", None),
        P(("groups", "seq")),
    )
    out_specs = P(("groups", "seq"), None)
    local = make_local(mesh.shape["seq"], mesh.shape["chan"])
    return jax.shard_map(local, mesh=mesh, in_specs=in_specs, out_specs=out_specs, check_vma=False)
```

profile of v0, /device:TPU:0, one launch (start us, length us, event | category | flops | bytes accessed | tf_op | source)
XLA Modules:
  0.0 107.2 jit_solution(14408337115999331326)
XLA Ops:
  0.0 1.1 %multiply_convert_fusion = bf16[128,1024]{1,0:T(8,128)(2,1)S(1)} fusion(bf16[128,1024]{1,0:T(8,128)(2,1)} %param.11, bf16[128,1024]{1,0:T(8,128)(2,1)} %param.12), kind=kLoop, calls=%fused_computation.59 | loop fusion | flops 524288 | bytes 786432 | tf_op jit(solution)/shard_map/convert_element_type | solution.py:84
  1.1 0.7 convert_element_type.56
  1.8 0.7 pad_maximum_fusion.10
  2.6 6.3 %all-to-all-start = ((bf16[4,144,256]{2,1,0:T(8,128)(2,1)}), bf16[4,144,256]{2,1,0:T(8,128)(2,1)S(1)}, u32[]{:S(2)}, u32[]{:S(2)}) async-start(bf16[4,144,256]{2,1,0:T(8,128)(2,1)} %pad_maximum_fusion.10), calls=%async_computation | async-start | bytes 589824 | tf_op jit(solution)/shard_map/all_to_all | solution.py:94
  8.9 0.7 dynamic-slice_bitcast_fusion
  9.7 1.4 %fusion.44 = f32[256,512]{0,1:T(8,128)S(1)} fusion(bf16[512,256]{0,1:T(8,128)(2,1)S(1)} %bitcast.85, bf16[512,512]{1,0:T(8,128)(2,1)} %constant.51.clone), kind=kOutput, calls=%fused_computation.93 | convolution fusion | flops 134217728 | bytes 1310720 | tf_op jit(solution)/shard_map/dot_general | solution.py:36
  11.1 1.4 %fusion.43 = f32[256,512]{0,1:T(8,128)S(1)} fusion(bf16[512,256]{0,1:T(8,128)(2,1)S(1)} %bitcast.87, bf16[512,512]{1,0:T(8,128)(2,1)} %constant.51.clone), kind=kOutput, calls=%fused_computation.92 | convolution fusion | flops 134217728 | bytes 1310720 | tf_op jit(solution)/shard_map/dot_general | solution.py:36
  12.5 1.4 %fusion.9 = f32[512,256]{1,0:T(8,128)S(1)} fusion(f32[256,512]{0,1:T(8,128)S(1)} %fusion.44, bf16[512,256]{0,1:T(8,128)(2,1)S(1)} %bitcast.86, bf16[512,512]{1,0:T(8,128)(2,1)} %constant.52.clone), kind=kOutput, calls=%fused_computation.22 | convolution fusion | flops 134348800 | bytes 1835008 | tf_op jit(solution)/shard_map/dot_general | solution.py:36
  13.8 1.4 %fusion.10 = f32[512,256]{1,0:T(8,128)S(1)} fusion(f32[256,512]{0,1:T(8,128)S(1)} %fusion.43, bf16[512,256]{0,1:T(8,128)(2,1)S(1)} %bitcast.88, bf16[512,512]{1,0:T(8,128)(2,1)} %constant.52.clone), kind=kOutput, calls=%fused_computation.24 | convolution fusion | flops 134348800 | bytes 1835008 | tf_op jit(solution)/shard_map/dot_general | solution.py:36
  15.2 0.0 copy-start.5
  15.2 0.0 copy-start.2
  15.3 0.0 copy-start.1
  15.3 14.6 %reshape_reshape.3 = bf16[4,256,2,2048]{3,2,1,0:T(2,128)(2,1)} reshape(bf16[1024,4096]{1,0:T(8,128)(2,1)} %param.16) | data formatting | bytes 16777216 | tf_op jit(solution)/shard_map/reshape;reshape | solution.py:117
  29.9 0.0 copy-done.5
  29.9 0.0 copy-start
  29.9 0.8 copy.40
  30.7 1.2 %slice_select_fusion.6 = (f32[256,256]{1,0:T(8,128)}, f32[256,256]{1,0:T(8,128)}, f32[256,256]{1,0:T(8,128)}, f32[256,256]{1,0:T(8,128)}, f32[256,256]{1,0:T(8,128)}, /*index=5*/f32[256,256]{1,0:T(8,128)}) fusion(f32[512,256]{1,0:T(8,128)S(1)} %fusion.10, pred[256]{0:T(512)(128)(4,1)S(1)} %iota_compare_fusion, f32[512,256]{1,0:T(8,128)S(1)} %fusion.9), kind=kLoop, calls=%fused_computation.70 | loop fusion | flops 262144 | bytes 2621696 | tf_op jit(solution)/shard_map/jit(_where)/select_n | solution.py:64
  32.0 0.0 all-to-all-done
  32.0 0.0 copy-start.3
  32.0 5.2 %all-to-all-start.1 = ((bf16[4,128,256]{1,2,0:T(8,128)(2,1)}), bf16[4,128,256]{1,2,0:T(8,128)(2,1)}, u32[]{:S(2)}, u32[]{:S(2)}) async-start(bf16[4,128,256]{1,2,0:T(8,128)(2,1)} %bitcast.90), calls=%async_computation.1 | async-start | bytes 524288 | tf_op jit(solution)/shard_map/all_to_all | solution.py:100
  37.2 0.1 copy.60
  37.4 0.0 copy-done.2
  37.4 0.5 fusion.29
  37.9 0.0 copy-done.1
  37.9 0.5 fusion.8
  38.4 1.6 %fusion.20 = (f32[256,512]{1,0:T(8,128)S(1)}, f32[256,512]{1,0:T(8,128)S(1)}) fusion(f32[256,256]{1,0:T(8,128)} %get-tuple-element.18, f32[256,256]{1,0:T(8,128)} %get-tuple-element.14, f32[512,512]{1,0:T(8,128)S(1)} %fusion.8, f32[256,256]{1,0:T(8,128)} %get-tuple-element.13), kind=kLoop, calls=%fused_computation.44 | loop fusion | flops 1179648 | bytes 2883584 | tf_op jit(solution)/shard_map/sub | solution.py:76
  40.0 0.0 copy-done
  40.1 0.0 copy-start.4
  40.1 0.5 fusion.30
  40.6 0.5 convolution_add_fusion.4
  41.1 0.0 copy-done.3
  41.1 0.5 fusion.7
  41.6 4.0 %all-to-all-done.1 = bf16[4,128,256]{1,2,0:T(8,128)(2,1)} async-done(((bf16[4,128,256]{1,2,0:T(8,128)(2,1)}), bf16[4,128,256]{1,2,0:T(8,128)(2,1)}, u32[]{:S(2)}, u32[]{:S(2)}) %all-to-all-start.1) | async-done | bytes 262176 | tf_op jit(solution)/shard_map/all_to_all | solution.py:100
  45.6 1.1 %broadcast_select_fusion.2 = (bf16[512,256]{0,1:T(8,128)(2,1)S(1)}, bf16[512,256]{0,1:T(8,128)(2,1)S(1)}) fusion(pred[512]{0:T(512)(128)(4,1)S(1)} %get-tuple-element.22, f32[512,512]{0,1:T(8,128)S(1)} %fusion.7, pred[512]{0:T(512)(128)(4,1)S(1)} %get-tuple-element.21, bf16[4,128,256]{1,2,0:T(8,128)(2,1)} %all-to-all-done.1), kind=kLoop, calls=%fused_computation.66 | loop fusion | flops 917504 | bytes 1836032 | tf_op jit(solution)/shard_map/jit(_where)/select_n | solution.py:72
  46.7 0.5 fusion.28
  47.2 0.5 fusion.6
  47.7 0.0 copy-done.4
  47.7 1.4 %fusion.24 = (f32[256,512]{1,0:T(8,128)S(1)}, f32[256,512]{1,0:T(8,128)S(1)}) fusion(f32[256,256]{1,0:T(8,128)S(1)} %copy-done.4, f32[256,256]{1,0:T(8,128)} %get-tuple-element.24, f32[512,512]{1,0:T(8,128)S(1)} %fusion.6, f32[256,256]{1,0:T(8,128)} %get-tuple-element.25), kind=kLoop, calls=%fused_computation.52 | loop fusion | flops 1179648 | bytes 2883584 | tf_op jit(solution)/shard_map/sub | solution.py:76
  49.1 0.5 fusion.31
  49.6 0.5 convolution_add_fusion.1
  50.1 0.5 fusion.5
  50.6 0.1 fusion.18
  50.8 0.8 copy.61
  51.6 3.6 %all-to-all-start.2 = ((bf16[4,128,256]{2,1,0:T(8,128)(2,1)}), bf16[4,128,256]{2,1,0:T(8,128)(2,1)S(1)}, u32[]{:S(2)}, u32[]{:S(2)}) async-start(bf16[4,128,256]{2,1,0:T(8,128)(2,1)} %bitcast.16), calls=%async_computation.2 | async-start | bytes 524288 | tf_op jit(solution)/shard_map/all_to_all | solution.py:104
  55.2 20.5 %constant_dynamic-slice_fusion = (bf16[4,256,1,2048]{3,2,1,0:T(2,128)(2,1)}, bf16[4,256,1,2048]{3,2,1,0:T(2,128)(2,1)}) fusion(bf16[4,256,2,2048]{3,2,1,0:T(2,128)(2,1)} %reshape_reshape.3, s32[]{:T(128)S(6)} %select_n.82, s32[]{:T(128)S(6)} %select_n.81), kind=kLoop, calls=%fused_computation.80 | loop fusion | bytes 16777224 | tf_op jit(solution)/shard_map/jit(dynamic_index_in_dim)/dynamic_slice | solution.py:118
  75.7 0.0 all-to-all-done.2
  75.7 6.0 %fusion.4 = bf16[128,2048]{1,0:T(8,128)(2,1)S(1)} fusion(bf16[4,128,256]{2,1,0:T(8,128)(2,1)S(1)} %all-to-all-done.2, bf16[4,256,1,2048]{3,2,1,0:T(2,128)(2,1)} %get-tuple-element.7), kind=kOutput, calls=%fused_computation.6 | convolution fusion | flops 537133056 | bytes 4980736 | tf_op jit(solution)/shard_map/dot_general | solution.py:109
  81.7 0.1 collective-permute-start
  81.8 1.9 %collective-permute-done = bf16[128,2048]{1,0:T(8,128)(2,1)S(1)} collective-permute-done((bf16[128,2048]{1,0:T(8,128)(2,1)S(1)}, bf16[128,2048]{1,0:T(8,128)(2,1)S(1)}, u32[]{:S(2)}, u32[]{:S(2)}) %collective-permute-start) | collective-permute-done | bytes 524320 | tf_op jit(solution)/shard_map/ppermute | solution.py:40
  83.7 6.1 %fusion.13 = (bf16[128,2048]{1,0:T(8,128)(2,1)S(1)}, f32[128,2048]{1,0:T(8,128)S(1)}) fusion(bf16[128,2048]{1,0:T(8,128)(2,1)S(1)} %collective-permute-done, bf16[4,128,256]{2,1,0:T(8,128)(2,1)S(1)} %all-to-all-done.2, bf16[4,256,1,2048]{3,2,1,0:T(2,128)(2,1)} %get-tuple-element.8), kind=kOutput, calls=%fused_computation.32 | convolution fusion | flops 537657344 | bytes 6553600 | tf_op jit(solution)/shard_map/dot_general | solution.py:109
  89.8 1.5 %collective-permute-start.1 = (bf16[128,2048]{1,0:T(8,128)(2,1)S(1)}, bf16[128,2048]{1,0:T(8,128)(2,1)S(1)}, u32[]{:S(2)}, u32[]{:S(2)}) collective-permute-start(bf16[128,2048]{1,0:T(8,128)(2,1)S(1)} %get-tuple-element.26), channel_id=1, source_target_pairs={{0,2},{1,3},{2,0},{3,1},{4,6},{5,7},{6,4},{7,5},{8,10},{9,11},{10,... | collective-permute-start | bytes 1572872 | tf_op jit(solution)/shard_map/ppermute | solution.py:40
  91.3 12.5 %collective-permute-done.1 = bf16[128,2048]{1,0:T(8,128)(2,1)S(1)} collective-permute-done((bf16[128,2048]{1,0:T(8,128)(2,1)S(1)}, bf16[128,2048]{1,0:T(8,128)(2,1)S(1)}, u32[]{:S(2)}, u32[]{:S(2)}) %collective-permute-start.1) | collective-permute-done | bytes 524320 | tf_op jit(solution)/shard_map/ppermute | solution.py:40
  103.8 0.2 add_convert_fusion
  104.0 0.1 collective-permute-start.2
  104.1 1.9 %collective-permute-done.2 = bf16[128,2048]{1,0:T(8,128)(2,1)S(1)} collective-permute-done((bf16[128,2048]{1,0:T(8,128)(2,1)S(1)}, bf16[128,2048]{1,0:T(8,128)(2,1)S(1)}, u32[]{:S(2)}, u32[]{:S(2)}) %collective-permute-start.2) | collective-permute-done | bytes 524320 | tf_op jit(solution)/shard_map/ppermute | solution.py:40
  106.0 1.2 %maximum_select_fusion = bf16[128,4096]{1,0:T(8,128)(2,1)} fusion(bf16[128,2048]{1,0:T(8,128)(2,1)S(1)} %collective-permute-done.2, bf16[128,2048]{1,0:T(8,128)(2,1)S(1)} %add_convert_fusion, pred[]{:T(512)S(6)} %eq.42), kind=kLoop, calls=%fused_computation.29 | loop fusion | flops 4718592 | bytes 2097153 | tf_op jit(solution)/shard_map/jit(_where)/select_n | solution.py:124
  (13 shorter events, 0.2 us)
Async XLA Ops:
  2.6 29.4 %all-to-all-start = ((bf16[4,144,256]{2,1,0:T(8,128)(2,1)}), bf16[4,144,256]{2,1,0:T(8,128)(2,1)S(1)}, u32[]{:S(2)}, u32[]{:S(2)}) async-start(bf16[4,144,256]{2,1,0:T(8,128)(2,1)} %pad_maximum_fusion.10), calls=%async_computation | async-start | bytes 589824 | tf_op jit(solution)/shard_map/all_to_all | solution.py:94
  15.2 14.6 %copy-start.5 = (bf16[128,1024]{1,0:T(8,128)(2,1)S(1)}, bf16[128,1024]{1,0:T(8,128)(2,1)}, u32[]{:S(2)}) copy-start(bf16[128,1024]{1,0:T(8,128)(2,1)} %param.13) | copy-start | bytes 786436
  15.2 22.2 %copy-start.2 = (bf16[512,512]{1,0:T(8,128)(2,1)S(1)}, bf16[512,512]{1,0:T(8,128)(2,1)}, u32[]{:S(2)}) copy-start(bf16[512,512]{1,0:T(8,128)(2,1)} %constant.51.clone) | copy-start | bytes 1572868
  15.3 22.7 %copy-start.1 = (bf16[512,512]{1,0:T(8,128)(2,1)S(1)}, bf16[512,512]{1,0:T(8,128)(2,1)}, u32[]{:S(2)}) copy-start(bf16[512,512]{1,0:T(8,128)(2,1)} %constant.52.clone) | copy-start | bytes 1572868
  29.9 10.2 %copy-start = (bf16[512,512]{1,0:T(8,128)(2,1)S(1)}, bf16[512,512]{1,0:T(8,128)(2,1)}, u32[]{:S(2)}) copy-start(bf16[512,512]{1,0:T(8,128)(2,1)} %constant.53.clone) | copy-start | bytes 1572868
  32.0 9.1 %copy-start.3 = (bf16[512,512]{1,0:T(8,128)(2,1)S(1)}, bf16[512,512]{1,0:T(8,128)(2,1)}, u32[]{:S(2)}) copy-start(bf16[512,512]{1,0:T(8,128)(2,1)} %constant.54.clone) | copy-start | bytes 1572868
  32.0 13.7 %all-to-all-start.1 = ((bf16[4,128,256]{1,2,0:T(8,128)(2,1)}), bf16[4,128,256]{1,2,0:T(8,128)(2,1)}, u32[]{:S(2)}, u32[]{:S(2)}) async-start(bf16[4,128,256]{1,2,0:T(8,128)(2,1)} %bitcast.90), calls=%async_computation.1 | async-start | bytes 524288 | tf_op jit(solution)/shard_map/all_to_all | solution.py:100
  40.1 7.6 %copy-start.4 = (f32[256,256]{1,0:T(8,128)S(1)}, f32[256,256]{1,0:T(8,128)}, u32[]{:S(2)}) copy-start(f32[256,256]{1,0:T(8,128)} %get-tuple-element.23) | copy-start | bytes 786436
  51.6 24.1 %all-to-all-start.2 = ((bf16[4,128,256]{2,1,0:T(8,128)(2,1)}), bf16[4,128,256]{2,1,0:T(8,128)(2,1)S(1)}, u32[]{:S(2)}, u32[]{:S(2)}) async-start(bf16[4,128,256]{2,1,0:T(8,128)(2,1)} %bitcast.16), calls=%async_computation.2 | async-start | bytes 524288 | tf_op jit(solution)/shard_map/all_to_all | solution.py:104
  81.7 2.0 %collective-permute-start = (bf16[128,2048]{1,0:T(8,128)(2,1)S(1)}, bf16[128,2048]{1,0:T(8,128)(2,1)S(1)}, u32[]{:S(2)}, u32[]{:S(2)}) collective-permute-start(bf16[128,2048]{1,0:T(8,128)(2,1)S(1)} %fusion.4), channel_id=1, source_target_pairs={{0,1},{1,0},{2,3},{3,2},{4,5},{5,4},{6,7},{7,6},{8,9},{9,8},{10,11... | collective-permute-start | bytes 1572872 | tf_op jit(solution)/shard_map/ppermute | solution.py:40
  89.8 14.0 %collective-permute-start.1 = (bf16[128,2048]{1,0:T(8,128)(2,1)S(1)}, bf16[128,2048]{1,0:T(8,128)(2,1)S(1)}, u32[]{:S(2)}, u32[]{:S(2)}) collective-permute-start(bf16[128,2048]{1,0:T(8,128)(2,1)S(1)} %get-tuple-element.26), channel_id=1, source_target_pairs={{0,2},{1,3},{2,0},{3,1},{4,6},{5,7},{6,4},{7,5},{8,10},{9,11},{10,... | collective-permute-start | bytes 1572872 | tf_op jit(solution)/shard_map/ppermute | solution.py:40
  104.0 2.0 %collective-permute-start.2 = (bf16[128,2048]{1,0:T(8,128)(2,1)S(1)}, bf16[128,2048]{1,0:T(8,128)(2,1)S(1)}, u32[]{:S(2)}, u32[]{:S(2)}) collective-permute-start(bf16[128,2048]{1,0:T(8,128)(2,1)S(1)} %add_convert_fusion), channel_id=1, source_target_pairs={{0,1},{1,0},{2,3},{3,2},{4,5},{5,4},{6,7},{7,6},{8,9},{9,8},{10,11... | collective-permute-start | bytes 1572872 | tf_op jit(solution)/shard_map/ppermute | solution.py:40
where the time goes:
time: 108 us; the launch traced here: 107 us
  local copies, waits for them, and re-layouts  37.8 us (35%)
  matrix products  22.4 us (21%)
  waiting for transfers between devices  20.3 us (19%)
  starting transfers between devices  16.8 us (16%)
  other arithmetic  9.49 us (9%)
    dynamic_slice x1, local copies, waits for them, and re-layouts, local(): lax.dynamic_index_in_dim(w_halves, 1 - core, 2, keepdims=False)  20.5 us
    ppermute x3, waiting for transfers between devices, swap(): return lax.ppermute(x, 'chan', [(c, c ^ bit) for c in range(4)])  16.3 us
    another operation x1, local copies, waits for them, and re-layouts, local(): w_halves = w_blocks.reshape(nseq, per, 2, width)  14.6 us
    dot_general x2, matrix products, project(): lax.dot_general(mix_blocks, w, (((0, 2), (0, 1)), ((), ())), preferred_el...  12.1 us
    dot_general x14, matrix products, mm(): return jnp.dot(a, b, preferred_element_type=F32)  10.3 us
    all_to_all x1, starting transfers between devices, local(): got = lax.all_to_all(payload, 'seq', 0, 0, tiled=True)  6.35 us
    all_to_all x1, starting transfers between devices, local(): lax.all_to_all(gate_blocks, 'seq', 0, 0, tiled=True)  5.22 us
    all_to_all x1, waiting for transfers between devices, local(): lax.all_to_all(gate_blocks, 'seq', 0, 0, tiled=True)  4.02 us
  transfers between devices with their start and end apart: 6, of which 4 were waited for; matrix products, arithmetic and copies ran while one was open for 45% of the time, Pallas kernels for 0%

commit v1 on v0

--- a/solution.py
+++ b/solution.py
@@ -6,6 +6,35 @@
 
 F32 = jnp.float32
 BF16 = jnp.bfloat16
+
+
+def roads_wrap(tile_in, in_dim, content):
+    spare = tile_in.shape
+    wide_out = tile_in.reshape(
+        *spare[:in_dim], content, spare[in_dim] // content, *spare[in_dim + 1 :]
+    )
+    return jnp.moveaxis(wide_out, in_dim, 0)
+
+
+def update_cells_all(w_in, ndim_at):
+    v_now = list(w_in.shape[1:])
+    v_now[ndim_at] *= w_in.shape[0]
+    return jnp.moveaxis(w_in, 0, ndim_at).reshape(v_now)
+
+
+def answer_array_on_mesh(own_rows, mine_x, row_axis, panel):
+    inter, lower = (jax.lax.axis_size(row_axis), jax.lax.axis_index(row_axis))
+    seen_now = roads_wrap(mine_x, own_rows, inter)
+    pages = [seen_now[lower]]
+    hop_no = 1
+    while hop_no < inter:
+        out_arr = seen_now[lower ^ hop_no]
+        pages.append(
+            jax.lax.ppermute(out_arr, row_axis, [(to_i, to_i ^ hop_no) for to_i in range(inter)])
+        )
+        hop_no += 1
+    seen_now = jnp.stack(pages)[lower ^ jnp.arange(inter)]
+    return update_cells_all(seen_now, panel)
 
 
 def split_bf16(mat):
@@ -97,7 +126,7 @@
         in0 = (segs == 0)[:, None]
         in1 = (segs == 1)[:, None]
         gate_blocks = second_gate.reshape(rows, nseq, per).transpose(1, 0, 2)
-        gate_cols = lax.all_to_all(gate_blocks, "seq", 0, 0, tiled=True).reshape(nseq * rows, per)
+        gate_cols = answer_array_on_mesh(0, gate_blocks, "seq", 0).reshape(nseq * rows, per)
         first_mix = long_conv(spectrum(first_filter), first_cols)
         second_input = (gate_cols.astype(F32) * first_mix).astype(BF16)
         second_mix = long_conv(spectrum(second_filter), second_input).astype(BF16)

time: 108 us -> 101 us (0.935)
  matrix products: 22.4 us -> 18.2 us
  waiting for transfers between devices: 20.3 us -> 16.3 us
  local copies, waits for them, and re-layouts: 37.8 us -> 39.3 us
  other arithmetic: 9.49 us -> 8.37 us
    all_to_all x1 -> x0, starting transfers between devices: 5.22 us -> none  [local(): lax.all_to_all(gate_blocks, 'seq', 0, 0, tiled=True)]
    ppermute x0 -> x3, starting transfers between devices: none -> 4.6 us  [answer_array_on_mesh(): jax.lax.ppermute(out_arr, row_axis, [(to_i, to_i ^ hop_no) for to_i in ra...]
    dot_general x14, matrix products: 10.3 us -> 6.16 us  [mm(): return jnp.dot(a, b, preferred_element_type=F32)]
    all_to_all x1 -> x0, waiting for transfers between devices: 4.02 us -> none  [local(): lax.all_to_all(gate_blocks, 'seq', 0, 0, tiled=True)]
    all_to_all x1, starting transfers between devices: 3.59 us -> 5.04 us  [local(): lax.all_to_all(second_mix.reshape(nseq, rows, per), 'seq', 0, 0, tiled=True)]
    sub x2, other arithmetic: 3.08 us -> 1.91 us  [long_conv(): y = jnp.concatenate([xr * a - xi * b, xr * b + xi * d], axis=0)]
  transfers between devices with their start and end apart: 6 -> 8, of which waited for: 4 -> 3; matrix products, arithmetic and copies ran while one was open for 45% -> 42% of each run, Pallas kernels for 0% -> 0%
where the time goes in v1:
time: 101 us; the launch traced here: 100 us
  local copies, waits for them, and re-layouts  39.3 us (39%)
  matrix products  18.2 us (18%)
  starting transfers between devices  17.7 us (18%)
  waiting for transfers between devices  16.3 us (16%)
  other arithmetic  8.37 us (8%)
    dynamic_slice x1, local copies, waits for them, and re-layouts, local(): lax.dynamic_index_in_dim(w_halves, 1 - core, 2, keepdims=False)  20.5 us
    ppermute x3, waiting for transfers between devices, swap(): return lax.ppermute(x, 'chan', [(c, c ^ bit) for c in range(4)])  16.3 us
    another operation x1, local copies, waits for them, and re-layouts, local(): w_halves = w_blocks.reshape(nseq, per, 2, width)  14.6 us
    dot_general x2, matrix products, project(): lax.dot_general(mix_blocks, w, (((0, 2), (0, 1)), ((), ())), preferred_el...  12.1 us
    all_to_all x1, starting transfers between devices, local(): got = lax.all_to_all(payload, 'seq', 0, 0, tiled=True)  6.35 us
    dot_general x14, matrix products, mm(): return jnp.dot(a, b, preferred_element_type=F32)  6.16 us
    all_to_all x1, starting transfers between devices, local(): lax.all_to_all(second_mix.reshape(nseq, rows, per), 'seq', 0, 0, tiled=True)  5.04 us
    ppermute x3, starting transfers between devices, answer_array_on_mesh(): jax.lax.ppermute(out_arr, row_axis, [(to_i, to_i ^ hop_no) for to_i in ra...  4.6 us
  transfers between devices with their start and end apart: 8, of which 3 were waited for; matrix products, arithmetic and copies ran while one was open for 42% of the time, Pallas kernels for 0%

profile of v1, /device:TPU:0, one launch (start us, length us, event | category | flops | bytes accessed | tf_op | source)
XLA Modules:
  0.0 100.4 jit_solution(7700127556647194926)
XLA Ops:
  0.0 1.1 %multiply_convert_fusion = bf16[128,1024]{1,0:T(8,128)(2,1)S(1)} fusion(bf16[128,1024]{1,0:T(8,128)(2,1)} %param.11, bf16[128,1024]{1,0:T(8,128)(2,1)} %param.12), kind=kLoop, calls=%fused_computation.59 | loop fusion | flops 524288 | bytes 786432 | tf_op jit(solution)/shard_map/convert_element_type | solution.py:113
  1.1 0.7 convert_element_type.56
  1.8 0.7 pad_maximum_fusion.10
  2.6 6.3 %all-to-all-start = ((bf16[4,144,256]{2,1,0:T(8,128)(2,1)}), bf16[4,144,256]{2,1,0:T(8,128)(2,1)S(1)}, u32[]{:S(2)}, u32[]{:S(2)}) async-start(bf16[4,144,256]{2,1,0:T(8,128)(2,1)} %pad_maximum_fusion.10), calls=%async_computation | async-start | bytes 589824 | tf_op jit(solution)/shard_map/all_to_all | solution.py:123
  8.9 1.1 %copy.40 = bf16[128,1024]{0,1:T(8,128)(2,1)S(1)} copy(bf16[128,1024]{1,0:T(8,128)(2,1)} %param.13) | data formatting | bytes 524288 | tf_op args[2]
  10.1 0.1 copy.42
  10.2 2.1 %collective-permute-start = (bf16[1,128,256]{2,1,0:T(8,128)(2,1)S(1)}, bf16[1,128,256]{2,1,0:T(8,128)(2,1)}, u32[]{:S(2)}, u32[]{:S(2)}) collective-permute-start(bf16[1,128,256]{2,1,0:T(8,128)(2,1)S(1)} %bitcast.98), channel_id=1, source_target_pairs={{0,4},{4,0},{8,12},{12,8},{1,5},{5,1},{9,13},{13,9},{2,6},{6,2},{1... | collective-permute-start | bytes 196616 | tf_op jit(solution)/shard_map/ppermute | solution.py:33
  12.3 0.1 copy.43
  12.4 2.4 %collective-permute-start.1 = (bf16[1,128,256]{2,1,0:T(8,128)(2,1)S(1)}, bf16[1,128,256]{2,1,0:T(8,128)(2,1)}, u32[]{:S(2)}, u32[]{:S(2)}) collective-permute-start(bf16[1,128,256]{2,1,0:T(8,128)(2,1)S(1)} %bitcast.99), channel_id=1, source_target_pairs={{0,8},{4,12},{8,0},{12,4},{1,9},{5,13},{9,1},{13,5},{2,10},{6,14},... | collective-permute-start | bytes 196616 | tf_op jit(solution)/shard_map/ppermute | solution.py:33
  14.8 0.1 copy.44
  14.9 0.1 collective-permute-start.2
  15.1 0.0 copy-start.2
  15.1 0.0 copy-start.1
  15.1 14.6 %reshape_reshape.4 = bf16[4,256,2,2048]{3,2,1,0:T(2,128)(2,1)} reshape(bf16[1024,4096]{1,0:T(8,128)(2,1)} %param.16) | data formatting | bytes 16777216 | tf_op jit(solution)/shard_map/reshape;reshape | solution.py:146
  29.7 0.7 dynamic-slice_bitcast_fusion.1
  30.4 0.0 copy-done.2
  30.5 0.3 fusion.46
  30.8 0.3 fusion.45
  31.2 0.0 copy-done.1
  31.2 0.3 fusion.9
  31.5 0.0 copy-start
  31.5 0.3 fusion.10
  31.9 0.1 copy.45
  32.0 1.2 %slice_select_fusion.6 = (f32[256,256]{1,0:T(8,128)}, f32[256,256]{1,0:T(8,128)}, f32[256,256]{1,0:T(8,128)}, f32[256,256]{1,0:T(8,128)S(1)}, f32[256,256]{1,0:T(8,128)}, /*index=5*/f32[256,256]{1,0:T(8,128)}) fusion(f32[512,256]{1,0:T(8,128)S(1)} %fusion.10, pred[256]{0:T(512)(128)(4,1)S(1)} %iota_compare_fusion, f32[512,256]{1,0:T(8,128)S(1)} %fusion.9), kind=kLoop, calls=%fused_computation.72 | loop fusion | flops 262144 | bytes 2621696 | tf_op jit(solution)/shard_map/jit(_where)/select_n | solution.py:93
  33.1 0.0 collective-permute-done
  33.2 0.0 collective-permute-done.1
  33.2 0.0 collective-permute-done.2
  33.2 0.9 maximum_bitcast_fusion
  34.1 0.6 gather_fusion
  34.7 0.1 bitcast_convert_fusion
  34.8 0.2 copy.67
  35.0 0.0 copy-start.3
  35.0 0.0 all-to-all-done
  35.1 0.1 copy.68
  35.3 0.5 fusion.30
  35.7 0.5 fusion.8
  36.2 1.7 %fusion.21 = (f32[256,512]{1,0:T(8,128)S(1)}, f32[256,512]{1,0:T(8,128)S(1)}) fusion(f32[256,256]{1,0:T(8,128)} %get-tuple-element.18, f32[256,256]{1,0:T(8,128)} %get-tuple-element.14, f32[512,512]{1,0:T(8,128)S(1)} %fusion.8, f32[256,256]{1,0:T(8,128)} %get-tuple-element.13), kind=kLoop, calls=%fused_computation.45 | loop fusion | flops 1179648 | bytes 2883584 | tf_op jit(solution)/shard_map/sub | solution.py:105
  37.9 0.0 copy-done
  37.9 0.0 copy-start.4
  37.9 0.5 fusion.31
  38.4 0.5 convolution_add_fusion.4
  38.9 0.5 fusion.7
  39.4 0.2 broadcast_select_fusion.2
  39.7 0.5 fusion.29
  40.1 0.5 fusion.6
  40.6 0.2 fusion.25
  40.9 0.5 fusion.32
  41.4 0.5 convolution_add_fusion.1
  41.9 0.5 fusion.5
  42.4 0.1 fusion.17
  42.5 0.8 copy.69
  43.3 5.0 %all-to-all-start.1 = ((bf16[4,128,256]{2,1,0:T(8,128)(2,1)}), bf16[4,128,256]{2,1,0:T(8,128)(2,1)S(1)}, u32[]{:S(2)}, u32[]{:S(2)}) async-start(bf16[4,128,256]{2,1,0:T(8,128)(2,1)} %bitcast.25), calls=%async_computation.1 | async-start | bytes 524288 | tf_op jit(solution)/shard_map/all_to_all | solution.py:133
  48.4 20.5 %constant_dynamic-slice_fusion = (bf16[4,256,1,2048]{3,2,1,0:T(2,128)(2,1)}, bf16[4,256,1,2048]{3,2,1,0:T(2,128)(2,1)}) fusion(bf16[4,256,2,2048]{3,2,1,0:T(2,128)(2,1)} %reshape_reshape.4, s32[]{:T(128)S(6)} %select_n.109, s32[]{:T(128)S(6)} %select_n.108), kind=kLoop, calls=%fused_computation.82 | loop fusion | bytes 16777224 | tf_op jit(solution)/shard_map/jit(dynamic_index_in_dim)/dynamic_slice | solution.py:147
  68.9 0.0 all-to-all-done.1
  68.9 6.0 %fusion.4 = bf16[128,2048]{1,0:T(8,128)(2,1)S(1)} fusion(bf16[4,128,256]{2,1,0:T(8,128)(2,1)S(1)} %all-to-all-done.1, bf16[4,256,1,2048]{3,2,1,0:T(2,128)(2,1)} %get-tuple-element.7), kind=kOutput, calls=%fused_computation.7 | convolution fusion | flops 537133056 | bytes 4980736 | tf_op jit(solution)/shard_map/dot_general | solution.py:138
  74.9 0.1 collective-permute-start.3
  75.0 1.9 %collective-permute-done.3 = bf16[128,2048]{1,0:T(8,128)(2,1)S(1)} collective-permute-done((bf16[128,2048]{1,0:T(8,128)(2,1)S(1)}, bf16[128,2048]{1,0:T(8,128)(2,1)S(1)}, u32[]{:S(2)}, u32[]{:S(2)}) %collective-permute-start.3) | collective-permute-done | bytes 524320 | tf_op jit(solution)/shard_map/ppermute | solution.py:69
  76.9 6.1 %fusion.13 = (bf16[128,2048]{1,0:T(8,128)(2,1)S(1)}, f32[128,2048]{1,0:T(8,128)S(1)}) fusion(bf16[128,2048]{1,0:T(8,128)(2,1)S(1)} %collective-permute-done.3, bf16[4,128,256]{2,1,0:T(8,128)(2,1)S(1)} %all-to-all-done.1, bf16[4,256,1,2048]{3,2,1,0:T(2,128)(2,1)} %get-tuple-element.8), kind=kOutput, calls=%fused_computation.33 | convolution fusion | flops 537657344 | bytes 6553600 | tf_op jit(solution)/shard_map/dot_general | solution.py:138
  82.9 1.6 %collective-permute-start.4 = (bf16[128,2048]{1,0:T(8,128)(2,1)S(1)}, bf16[128,2048]{1,0:T(8,128)(2,1)S(1)}, u32[]{:S(2)}, u32[]{:S(2)}) collective-permute-start(bf16[128,2048]{1,0:T(8,128)(2,1)S(1)} %get-tuple-element.30), channel_id=1, source_target_pairs={{0,2},{1,3},{2,0},{3,1},{4,6},{5,7},{6,4},{7,5},{8,10},{9,11},{10,... | collective-permute-start | bytes 1572872 | tf_op jit(solution)/shard_map/ppermute | solution.py:69
  84.5 12.5 %collective-permute-done.4 = bf16[128,2048]{1,0:T(8,128)(2,1)S(1)} collective-permute-done((bf16[128,2048]{1,0:T(8,128)(2,1)S(1)}, bf16[128,2048]{1,0:T(8,128)(2,1)S(1)}, u32[]{:S(2)}, u32[]{:S(2)}) %collective-permute-start.4) | collective-permute-done | bytes 524320 | tf_op jit(solution)/shard_map/ppermute | solution.py:69
  97.0 0.2 add_convert_fusion
  97.2 0.1 collective-permute-start.5
  97.3 1.9 %collective-permute-done.5 = bf16[128,2048]{1,0:T(8,128)(2,1)S(1)} collective-permute-done((bf16[128,2048]{1,0:T(8,128)(2,1)S(1)}, bf16[128,2048]{1,0:T(8,128)(2,1)S(1)}, u32[]{:S(2)}, u32[]{:S(2)}) %collective-permute-start.5) | collective-permute-done | bytes 524320 | tf_op jit(solution)/shard_map/ppermute | solution.py:69
  99.2 1.2 %maximum_select_fusion = bf16[128,4096]{1,0:T(8,128)(2,1)} fusion(bf16[128,2048]{1,0:T(8,128)(2,1)S(1)} %collective-permute-done.5, bf16[128,2048]{1,0:T(8,128)(2,1)S(1)} %add_convert_fusion, pred[]{:T(512)S(6)} %eq.42), kind=kLoop, calls=%fused_computation.30 | loop fusion | flops 4718592 | bytes 2097153 | tf_op jit(solution)/shard_map/jit(_where)/select_n | solution.py:153
  (20 shorter events, 0.3 us)
Async XLA Ops:
  2.6 32.4 %all-to-all-start = ((bf16[4,144,256]{2,1,0:T(8,128)(2,1)}), bf16[4,144,256]{2,1,0:T(8,128)(2,1)S(1)}, u32[]{:S(2)}, u32[]{:S(2)}) async-start(bf16[4,144,256]{2,1,0:T(8,128)(2,1)} %pad_maximum_fusion.10), calls=%async_computation | async-start | bytes 589824 | tf_op jit(solution)/shard_map/all_to_all | solution.py:123
  10.2 23.0 %collective-permute-start = (bf16[1,128,256]{2,1,0:T(8,128)(2,1)S(1)}, bf16[1,128,256]{2,1,0:T(8,128)(2,1)}, u32[]{:S(2)}, u32[]{:S(2)}) collective-permute-start(bf16[1,128,256]{2,1,0:T(8,128)(2,1)S(1)} %bitcast.98), channel_id=1, source_target_pairs={{0,4},{4,0},{8,12},{12,8},{1,5},{5,1},{9,13},{13,9},{2,6},{6,2},{1... | collective-permute-start | bytes 196616 | tf_op jit(solution)/shard_map/ppermute | solution.py:33
  12.4 20.8 %collective-permute-start.1 = (bf16[1,128,256]{2,1,0:T(8,128)(2,1)S(1)}, bf16[1,128,256]{2,1,0:T(8,128)(2,1)}, u32[]{:S(2)}, u32[]{:S(2)}) collective-permute-start(bf16[1,128,256]{2,1,0:T(8,128)(2,1)S(1)} %bitcast.99), channel_id=1, source_target_pairs={{0,8},{4,12},{8,0},{12,4},{1,9},{5,13},{9,1},{13,5},{2,10},{6,14},... | collective-permute-start | bytes 196616 | tf_op jit(solution)/shard_map/ppermute | solution.py:33
  14.9 18.2 %collective-permute-start.2 = (bf16[1,128,256]{2,1,0:T(8,128)(2,1)S(1)}, bf16[1,128,256]{2,1,0:T(8,128)(2,1)}, u32[]{:S(2)}, u32[]{:S(2)}) collective-permute-start(bf16[1,128,256]{2,1,0:T(8,128)(2,1)S(1)} %bitcast.100), channel_id=1, source_target_pairs={{0,12},{4,8},{8,4},{12,0},{1,13},{5,9},{9,5},{13,1},{2,14},{6,10},... | collective-permute-start | bytes 196616 | tf_op jit(solution)/shard_map/ppermute | solution.py:33
  15.1 15.4 %copy-start.2 = (bf16[512,512]{1,0:T(8,128)(2,1)S(1)}, bf16[512,512]{1,0:T(8,128)(2,1)}, u32[]{:S(2)}) copy-start(bf16[512,512]{1,0:T(8,128)(2,1)} %constant.56.clone) | copy-start | bytes 1572868
  15.1 16.1 %copy-start.1 = (bf16[512,512]{1,0:T(8,128)(2,1)S(1)}, bf16[512,512]{1,0:T(8,128)(2,1)}, u32[]{:S(2)}) copy-start(bf16[512,512]{1,0:T(8,128)(2,1)} %constant.57.clone) | copy-start | bytes 1572868
  31.5 6.4 %copy-start = (bf16[512,512]{1,0:T(8,128)(2,1)S(1)}, bf16[512,512]{1,0:T(8,128)(2,1)}, u32[]{:S(2)}) copy-start(bf16[512,512]{1,0:T(8,128)(2,1)} %constant.58.clone) | copy-start | bytes 1572868
  35.0 4.0 %copy-start.3 = (bf16[512,512]{1,0:T(8,128)(2,1)S(1)}, bf16[512,512]{1,0:T(8,128)(2,1)}, u32[]{:S(2)}) copy-start(bf16[512,512]{1,0:T(8,128)(2,1)} %constant.59.clone) | copy-start | bytes 1572868
  37.9 2.7 %copy-start.4 = (f32[256,256]{1,0:T(8,128)S(1)}, f32[256,256]{1,0:T(8,128)}, u32[]{:S(2)}) copy-start(f32[256,256]{1,0:T(8,128)} %get-tuple-element.28) | copy-start | bytes 786436
  37.9 2.7 %copy-start.5 = (f32[256,256]{1,0:T(8,128)S(1)}, f32[256,256]{1,0:T(8,128)}, u32[]{:S(2)}) copy-start(f32[256,256]{1,0:T(8,128)} %get-tuple-element.29) | copy-start | bytes 786436
  43.3 25.5 %all-to-all-start.1 = ((bf16[4,128,256]{2,1,0:T(8,128)(2,1)}), bf16[4,128,256]{2,1,0:T(8,128)(2,1)S(1)}, u32[]{:S(2)}, u32[]{:S(2)}) async-start(bf16[4,128,256]{2,1,0:T(8,128)(2,1)} %bitcast.25), calls=%async_computation.1 | async-start | bytes 524288 | tf_op jit(solution)/shard_map/all_to_all | solution.py:133
  74.9 2.0 %collective-permute-start.3 = (bf16[128,2048]{1,0:T(8,128)(2,1)S(1)}, bf16[128,2048]{1,0:T(8,128)(2,1)S(1)}, u32[]{:S(2)}, u32[]{:S(2)}) collective-permute-start(bf16[128,2048]{1,0:T(8,128)(2,1)S(1)} %fusion.4), channel_id=1, source_target_pairs={{0,1},{1,0},{2,3},{3,2},{4,5},{5,4},{6,7},{7,6},{8,9},{9,8},{10,11... | collective-permute-start | bytes 1572872 | tf_op jit(solution)/shard_map/ppermute | solution.py:69
  82.9 14.0 %collective-permute-start.4 = (bf16[128,2048]{1,0:T(8,128)(2,1)S(1)}, bf16[128,2048]{1,0:T(8,128)(2,1)S(1)}, u32[]{:S(2)}, u32[]{:S(2)}) collective-permute-start(bf16[128,2048]{1,0:T(8,128)(2,1)S(1)} %get-tuple-element.30), channel_id=1, source_target_pairs={{0,2},{1,3},{2,0},{3,1},{4,6},{5,7},{6,4},{7,5},{8,10},{9,11},{10,... | collective-permute-start | bytes 1572872 | tf_op jit(solution)/shard_map/ppermute | solution.py:69
  97.2 2.0 %collective-permute-start.5 = (bf16[128,2048]{1,0:T(8,128)(2,1)S(1)}, bf16[128,2048]{1,0:T(8,128)(2,1)S(1)}, u32[]{:S(2)}, u32[]{:S(2)}) collective-permute-start(bf16[128,2048]{1,0:T(8,128)(2,1)S(1)} %add_convert_fusion), channel_id=1, source_target_pairs={{0,1},{1,0},{2,3},{3,2},{4,5},{5,4},{6,7},{7,6},{8,9},{9,8},{10,11... | collective-permute-start | bytes 1572872 | tf_op jit(solution)/shard_map/ppermute | solution.py:69
